TPU v7x, 32 devices: a whole 2x2x4 slice. The times are simulated.
32 devices in a mesh: rep: 4 (over y, core), ep: 8 (over z, x).
Axes of the slice: x: 2, y: 2, z: 4, core: 2. Of those that a mesh axis runs over, the one named last changes fastest.
Arguments:
- tokens: bfloat16 [8192, 2048], P(('rep', 'ep')), may hold values from -6 to 6
- expert_ids: int32 [8192, 8], P(('rep', 'ep')), may hold values from 0 to 127, as said below
- gate_weights: float32 [8192, 8], P(('rep', 'ep')), may hold values from 0.25 to 1
- w_gate: bfloat16 [8, 768, 2048], P('ep'), may hold values from -0.125 to 0.125
- w_up: bfloat16 [8, 768, 2048], P('ep'), may hold values from -0.125 to 0.125
- w_down: bfloat16 [8, 768, 2048], P('ep'), may hold values from -0.21875 to 0.21875
- out_grad: bfloat16 [8192, 2048], P(('rep', 'ep')), may hold values from -6 to 6
Outputs:
- layer_out: bfloat16 [8192, 2048], P(('rep', 'ep'))
- tokens_grad: bfloat16 [8192, 2048], P(('rep', 'ep'))
- gates_grad: float32 [8192, 8], P(('rep', 'ep'))
- gate_w_grad: bfloat16 [8, 768, 2048], P('ep', 'rep')
- up_w_grad: bfloat16 [8, 768, 2048], P('ep', 'rep')
- down_w_grad: bfloat16 [8, 768, 2048], P('ep', 'rep')
Inputs may be any that keep to these rules, and one draw needn't show every extreme that they name: `expert_ids`: entry j of a row lies in [16 * j, 16 * j + 16); in the rows of one device no id below 8 appears more than 32 times, and some id below 8 appears exactly 32 times.
All inputs are finite; a program needn't handle non-finite values.
Results may differ from a plain program's by a relative error of at most 0.0065.
Values may be sent and summed in bfloat16 or wider, within the bound.
No kernel may reach another device: no remote copies, remote signals or barrier semaphores. Data moves between devices by JAX's collectives and lax.ppermute only.
A program may use at most 128 MiB of HBM per device.

v0:
```python
import jax
import jax.numpy as jnp
from jax import lax
from jax.sharding import PartitionSpec as P

STRIPE = 16


def silu_grad(value):
    sigmoid_value = jax.nn.sigmoid(value)
    return sigmoid_value * (1.0 + value * (1.0 - sigmoid_value))


def rows_times(left, right):
    return lax.dot_general(
        left, right, (((1,), (1,)), ((), ())), preferred_element_type=jnp.float32
    )


def inner_rows(left, right):
    return lax.dot_general(
        left, right, (((0,), (0,)), ((), ())), preferred_element_type=jnp.float32
    )


def matmul(left, right):
    return jnp.dot(left, right, preferred_element_type=jnp.float32)


def body(tokens, expert_ids, gate_weights, w_gate, w_up, w_down, out_grad):
    tok_count, feature_width = tokens.shape
    top_count = expert_ids.shape[1]
    experts = lax.axis_size("ep")
    per_pair = tok_count // 8
    total_slots = experts * per_pair
    live_cols = min(top_count, -(-experts // STRIPE))
    assigned = tok_count * live_cols
    flat_ids = expert_ids[:, :live_cols].reshape(-1)
    flat_gates = gate_weights[:, :live_cols].reshape(-1)
    live_mask = flat_ids < experts
    onehot = flat_ids[:, None] == jnp.arange(experts, dtype=jnp.int32)[None, :]
    position = jnp.arange(assigned, dtype=jnp.int32)
    earlier = (position[:, None] > position[None, :]).astype(jnp.bfloat16)
    before = matmul(earlier, onehot.astype(jnp.bfloat16))
    slot_rank = jnp.sum(jnp.where(onehot, before, 0.0), axis=1).astype(jnp.int32)
    slot_index = jnp.where(live_mask, flat_ids * per_pair + slot_rank, -1)
    slot_ids = jnp.arange(total_slots, dtype=jnp.int32)
    hit = slot_ids[:, None] == slot_index[None, :]
    slot_gate = jnp.sum(jnp.where(hit, flat_gates[None, :], 0.0), axis=1)
    pick = jnp.any(hit.reshape(total_slots, tok_count, live_cols), axis=2).astype(jnp.bfloat16)
    send_rows = matmul(pick, tokens).astype(jnp.bfloat16)
    grad_rows = matmul(pick, out_grad)
    scaled_grad = (slot_gate[:, None] * grad_rows).astype(jnp.bfloat16)

    def exchange(rows):
        return lax.all_to_all(
            rows.reshape(experts, per_pair, feature_width),
            "ep",
            split_axis=0,
            concat_axis=0,
            tiled=True,
        ).reshape(total_slots, feature_width)

    rows_in = exchange(send_rows)
    grad_in = exchange(scaled_grad)
    copies = lax.axis_size("rep")
    by_pieces = copies == 4

    def to_copy(values, step):
        return lax.ppermute(values, "rep", [(r, r ^ step) for r in range(copies)])

    if by_pieces:
        far_rows = to_copy(rows_in, 2)
        near_rows = to_copy(rows_in, 1)
    else:
        gathered_rows = lax.all_gather(rows_in, "rep", axis=0, tiled=True)
        gathered_grad = lax.all_gather(grad_in, "rep", axis=0, tiled=True)
    gate_mat = w_gate[0]
    up_mat = w_up[0]
    down_mat = w_down[0]
    gate_up_mat = jnp.concatenate([gate_mat, up_mat], axis=0)
    hidden_units = gate_mat.shape[0]
    pre_both_own = rows_times(rows_in, gate_up_mat)
    pre_gate = pre_both_own[:, :hidden_units]
    pre_up = pre_both_own[:, hidden_units:]
    activated = jax.nn.silu(pre_gate)
    hidden = (activated * pre_up).astype(jnp.bfloat16)
    expert_out = matmul(hidden, down_mat).astype(jnp.bfloat16)
    expert_out, grad_in = lax.optimization_barrier((expert_out, grad_in))
    returned = lax.all_to_all(
        expert_out.reshape(experts, per_pair, feature_width),
        "ep",
        split_axis=0,
        concat_axis=0,
        tiled=True,
    ).reshape(total_slots, feature_width)
    hidden_grad = rows_times(grad_in, down_mat)
    gate_pre_grad = (hidden_grad * pre_up * silu_grad(pre_gate)).astype(jnp.bfloat16)
    up_pre_grad = (hidden_grad * activated).astype(jnp.bfloat16)
    token_part = matmul(jnp.concatenate([gate_pre_grad, up_pre_grad], axis=1), gate_up_mat).astype(
        jnp.bfloat16
    )
    if by_pieces:
        token_part, grad_out = lax.optimization_barrier((token_part, grad_in))
        far_grad = to_copy(grad_out, 2)
        near_grad = to_copy(grad_out, 1)
    part_back = lax.all_to_all(
        token_part.reshape(experts, per_pair, feature_width),
        "ep",
        split_axis=0,
        concat_axis=0,
        tiled=True,
    ).reshape(total_slots, feature_width)
    if by_pieces:
        returned, near_rows, near_grad = lax.optimization_barrier((returned, near_rows, near_grad))
    slot_grid = slot_index.reshape(tok_count, live_cols)
    gate_grid = flat_gates.reshape(tok_count, live_cols)
    layer_sum = jnp.zeros((tok_count, feature_width), jnp.float32)
    gate_cols = []
    back_pick = jnp.zeros((tok_count, total_slots), jnp.bfloat16)
    for col in range(live_cols):
        col_pick = (slot_grid[:, col : col + 1] == slot_ids[None, :]).astype(jnp.bfloat16)
        back_pick = back_pick + col_pick
        out_rows = matmul(col_pick, returned)
        layer_sum = layer_sum + gate_grid[:, col : col + 1] * out_rows
        gate_cols.append(jnp.sum(out_grad.astype(jnp.float32) * out_rows, axis=1))
    if by_pieces:
        layer_sum, far_rows, far_grad = lax.optimization_barrier((layer_sum, far_rows, far_grad))
        pieces = [
            (rows_in, grad_in),
            (near_rows, near_grad),
            (far_rows, far_grad),
            (to_copy(far_rows, 1), to_copy(far_grad, 1)),
        ]
    else:
        pieces = [(gathered_rows, gathered_grad)]
    layer_out = layer_sum.astype(jnp.bfloat16)
    gate_cols.extend([jnp.zeros((tok_count,), jnp.float32)] * (top_count - live_cols))
    gates_grad = jnp.stack(gate_cols, axis=1)
    share = gate_mat.shape[0] // copies
    start = lax.axis_index("rep") * share
    gate_share = lax.dynamic_slice_in_dim(gate_mat, start, share, axis=0)
    up_share = lax.dynamic_slice_in_dim(up_mat, start, share, axis=0)
    down_share = lax.dynamic_slice_in_dim(down_mat, start, share, axis=0)
    both_sum = None
    down_sum = None
    stacked_share = jnp.concatenate([gate_share, up_share], axis=0)
    for rows_p, grad_p in pieces:
        pre_both = rows_times(rows_p, stacked_share)
        pre_gate_s = pre_both[:, :share]
        pre_up_s = pre_both[:, share:]
        activated_s = jax.nn.silu(pre_gate_s)
        hidden_s = (activated_s * pre_up_s).astype(jnp.bfloat16)
        hidden_grad_s = rows_times(grad_p, down_share)
        gate_pre_grad_s = (hidden_grad_s * pre_up_s * silu_grad(pre_gate_s)).astype(jnp.bfloat16)
        up_pre_grad_s = (hidden_grad_s * activated_s).astype(jnp.bfloat16)
        both_p = inner_rows(jnp.concatenate([gate_pre_grad_s, up_pre_grad_s], axis=1), rows_p)
        down_p = inner_rows(hidden_s, grad_p)
        both_sum = both_p if both_sum is None else both_sum + both_p
        down_sum = down_p if down_sum is None else down_sum + down_p
    gate_w_grad = both_sum[:share].astype(jnp.bfloat16)[None]
    up_w_grad = both_sum[share:].astype(jnp.bfloat16)[None]
    down_w_grad = down_sum.astype(jnp.bfloat16)[None]
    part_back, gate_w_grad, up_w_grad, down_w_grad = lax.optimization_barrier(
        (part_back, gate_w_grad, up_w_grad, down_w_grad)
    )
    tokens_grad = matmul(back_pick, part_back).astype(jnp.bfloat16)
    return (layer_out, tokens_grad, gates_grad, gate_w_grad, up_w_grad, down_w_grad)


def solution(mesh):
    return jax.shard_map(
        body,
        mesh=mesh,
        in_specs=(
            P(("rep", "ep"), None),
            P(("rep", "ep"), None),
            P(("rep", "ep"), None),
            P("ep", None, None),
            P("ep", None, None),
            P("ep", None, None),
            P(("rep", "ep"), None),
        ),
        out_specs=(
            P(("rep", "ep"), None),
            P(("rep", "ep"), None),
            P(("rep", "ep"), None),
            P("ep", "rep", None),
            P("ep", "rep", None),
            P("ep", "rep", None),
        ),
        check_vma=False,
    )
```

profile of v0, /device:TPU:0, one launch (start us, length us, event | category | flops | bytes accessed | tf_op | source)
XLA Modules:
  0.0 129.3 jit_solution(9352168649783690748)
XLA Ops:
  0.6 0.9 slice.45
  1.5 0.2 fusion.14
  1.7 2.6 %convolution_convert_fusion.1 = bf16[256,2048]{1,0:T(8,128)(2,1)} fusion(bf16[256,2048]{1,0:T(8,128)(2,1)} %param.7, s32[256]{0:T(256)S(1)} %compare_select_fusion.1), kind=kOutput, calls=%fused_computation.14 | convolution fusion | flops 269025280 | bytes 2098176 | tf_op jit(solution)/shard_map/dot_general | solution.py:27
  4.4 7.3 %all-to-all-start = ((bf16[8,32,2048]{2,1,0:T(8,128)(2,1)}), bf16[8,32,2048]{2,1,0:T(8,128)(2,1)}, u32[]{:S(2)}, u32[]{:S(2)}) async-start(bf16[8,32,2048]{2,1,0:T(8,128)(2,1)} %bitcast.75), calls=%async_computation | async-start | bytes 2097152 | tf_op jit(solution)/shard_map/all_to_all | solution.py:56
  11.6 0.7 slice.44
  12.3 0.1 select_reduce_fusion
  12.4 2.6 %fusion.6 = bf16[256,2048]{1,0:T(8,128)(2,1)} fusion(bf16[256,2048]{1,0:T(8,128)(2,1)} %param.13, f32[256]{0:T(256)S(1)} %select_reduce_fusion, s32[256]{0:T(256)S(1)} %compare_select_fusion.1), kind=kOutput, calls=%fused_computation.11 | convolution fusion | flops 269549568 | bytes 2099200 | tf_op jit(solution)/shard_map/dot_general | solution.py:27
  15.1 22.4 %all-to-all-done = bf16[8,32,2048]{2,1,0:T(8,128)(2,1)} async-done(((bf16[8,32,2048]{2,1,0:T(8,128)(2,1)}), bf16[8,32,2048]{2,1,0:T(8,128)(2,1)}, u32[]{:S(2)}, u32[]{:S(2)}) %all-to-all-start) | async-done | bytes 1048608 | tf_op jit(solution)/shard_map/all_to_all | solution.py:56
  37.5 4.3 %all-to-all-start.1 = ((bf16[8,32,2048]{2,1,0:T(8,128)(2,1)}), bf16[8,32,2048]{2,1,0:T(8,128)(2,1)}, u32[]{:S(2)}, u32[]{:S(2)}) async-start(bf16[8,32,2048]{2,1,0:T(8,128)(2,1)} %bitcast.74), calls=%async_computation.1 | async-start | bytes 2097152 | tf_op jit(solution)/shard_map/all_to_all | solution.py:56
  41.9 0.1 pad.3.clone
  41.9 0.1 pad.2.clone
  42.0 0.9 compare_select_fusion
  42.9 2.8 %dynamic-slice_bitcast_fusion = (bf16[192,2048]{1,0:T(8,128)(2,1)}, bf16[192,2048]{1,0:T(8,128)(2,1)}) fusion(bf16[1,768,2048]{2,1,0:T(8,128)(2,1)} %param.11, s32[]{:T(128)S(6)} %select_n.28, bf16[1,768,2048]{2,1,0:T(8,128)(2,1)} %param.10), kind=kLoop, calls=%fused_computation.37 | loop fusion | bytes 3145732 | tf_op jit(solution)/shard_map/dynamic_slice | solution.py:143
  45.7 1.5 %collective-permute-start.2 = (bf16[256,2048]{1,0:T(8,128)(2,1)}, bf16[256,2048]{1,0:T(8,128)(2,1)}, u32[]{:S(2)}, u32[]{:S(2)}) collective-permute-start(bf16[256,2048]{1,0:T(8,128)(2,1)} %bitcast.5), channel_id=1, source_target_pairs={{0,16},{8,24},{16,0},{24,8},{1,17},{9,25},{17,1},{25,9},{2,18},{10... | collective-permute-start | bytes 3145736 | tf_op jit(solution)/shard_map/ppermute | solution.py:70
  47.2 4.0 %fusion.1 = f32[256,1536]{1,0:T(8,128)S(1)} fusion(bf16[256,2048]{1,0:T(8,128)(2,1)} %bitcast.5, bf16[768,2048]{1,0:T(8,128)(2,1)S(1)} %bitcast.78, bf16[768,2048]{1,0:T(8,128)(2,1)} %bitcast.80), kind=kOutput, calls=%fused_computation.2 | convolution fusion | flops 1623195648 | bytes 8912896 | tf_op jit(solution)/shard_map/dot_general | solution.py:15
  51.2 1.2 copy-done.11
  52.4 2.0 %fusion.9 = bf16[256,2048]{1,0:T(8,128)(2,1)} fusion(bf16[1,768,2048]{2,1,0:T(8,128)(2,1)S(1)} %copy-done, f32[256,1536]{1,0:T(8,128)S(1)} %fusion.1), kind=kOutput, calls=%fused_computation.16 | convolution fusion | flops 807010304 | bytes 5767168 | tf_op jit(solution)/shard_map/dot_general | solution.py:27
  54.4 12.9 %all-to-all-done.1 = bf16[8,32,2048]{2,1,0:T(8,128)(2,1)} async-done(((bf16[8,32,2048]{2,1,0:T(8,128)(2,1)}), bf16[8,32,2048]{2,1,0:T(8,128)(2,1)}, u32[]{:S(2)}, u32[]{:S(2)}) %all-to-all-start.1) | async-done | bytes 1048608 | tf_op jit(solution)/shard_map/all_to_all | solution.py:56
  67.3 4.2 %all-to-all-start.2 = ((bf16[8,32,2048]{2,1,0:T(8,128)(2,1)}), bf16[8,32,2048]{2,1,0:T(8,128)(2,1)}, u32[]{:S(2)}, u32[]{:S(2)}) async-start(bf16[8,32,2048]{2,1,0:T(8,128)(2,1)} %bitcast.77), calls=%async_computation.2 | async-start | bytes 2097152 | tf_op jit(solution)/shard_map/all_to_all | solution.py:90
  71.6 3.0 %multiply_convert_fusion.1 = (bf16[256,768]{1,0:T(8,128)(2,1)S(1)}, bf16[256,768]{1,0:T(8,128)(2,1)S(1)}) fusion(f32[256,1536]{1,0:T(8,128)} %copy-done.11, bf16[256,2048]{1,0:T(8,128)(2,1)} %bitcast.10, bf16[1,768,2048]{2,1,0:T(8,128)(2,1)S(1)} %copy-done), kind=kOutput, calls=%fused_computation.40 | convolution fusion | flops 807862272 | bytes 6553600 | tf_op jit(solution)/shard_map/dot_general | solution.py:15
  74.7 0.6 copy-done.10
  75.2 2.8 %fusion.7 = bf16[256,2048]{1,0:T(8,128)(2,1)} fusion(bf16[768,2048]{1,0:T(8,128)(2,1)S(1)} %bitcast.79, bf16[768,2048]{1,0:T(8,128)(2,1)S(1)} %bitcast.81, bf16[256,768]{1,0:T(8,128)(2,1)S(1)} %get-tuple-element.35, bf16[256,768]{1,0:T(8,128)(2,1)S(1)} %get-tuple-element.34), kind=kOutput, calls=%fused_computation.12 | convolution fusion | flops 1625292800 | bytes 8126464 | tf_op jit(solution)/shard_map/dot_general | solution.py:27
  78.1 1.5 %collective-permute-start.3 = (bf16[256,2048]{1,0:T(8,128)(2,1)}, bf16[256,2048]{1,0:T(8,128)(2,1)}, u32[]{:S(2)}, u32[]{:S(2)}) collective-permute-start(bf16[256,2048]{1,0:T(8,128)(2,1)} %bitcast.10), channel_id=1, source_target_pairs={{0,16},{8,24},{16,0},{24,8},{1,17},{9,25},{17,1},{25,9},{2,18},{10... | collective-permute-start | bytes 3145736 | tf_op jit(solution)/shard_map/ppermute | solution.py:70
  79.6 1.8 %fusion.84 = f32[256,384]{0,1:T(8,128)S(1)} fusion(bf16[256,2048]{1,0:T(8,128)(2,1)} %bitcast.5, bf16[192,2048]{1,0:T(8,128)(2,1)S(1)} %copy-done.4, bf16[192,2048]{1,0:T(8,128)(2,1)S(1)} %copy-done.6), kind=kOutput, calls=%fused_computation.118 | convolution fusion | flops 405798912 | bytes 3014656 | tf_op jit(solution)/shard_map/dot_general | solution.py:15
  81.4 1.7 %multiply_convert_fusion.15 = (bf16[256,192]{0,1:T(8,128)(2,1)S(1)}, bf16[256,192]{0,1:T(8,128)(2,1)S(1)}) fusion(f32[256,384]{0,1:T(8,128)S(1)} %fusion.84, bf16[256,2048]{1,0:T(8,128)(2,1)} %bitcast.10, bf16[1,768,2048]{2,1,0:T(8,128)(2,1)S(1)} %copy-done, s32[]{:T(128)S(6)} %select_n.28), kind=kOutput, calls=%fused_computation.86 | convolution fusion | flops 201965568 | bytes 2424836 | tf_op jit(solution)/shard_map/dot_general | solution.py:15
  83.2 2.8 %fusion.58 = f32[192,2048]{1,0:T(8,128)} fusion(bf16[256,2048]{1,0:T(8,128)(2,1)} %bitcast.10, f32[256,384]{0,1:T(8,128)S(1)} %fusion.84), kind=kOutput, calls=%fused_computation.93 | convolution fusion | flops 201621504 | bytes 3014656 | tf_op jit(solution)/shard_map/dot_general | solution.py:21
  85.9 3.4 %fusion.32 = f32[384,2048]{1,0:T(8,128)} fusion(bf16[256,2048]{1,0:T(8,128)(2,1)} %bitcast.5, bf16[256,192]{0,1:T(8,128)(2,1)S(1)} %get-tuple-element.43, bf16[256,192]{0,1:T(8,128)(2,1)S(1)} %get-tuple-element.42), kind=kOutput, calls=%fused_computation.53 | convolution fusion | flops 403046400 | bytes 4390912 | tf_op jit(solution)/shard_map/dot_general | solution.py:21
  89.4 7.6 %all-to-all-done.2 = bf16[8,32,2048]{2,1,0:T(8,128)(2,1)} async-done(((bf16[8,32,2048]{2,1,0:T(8,128)(2,1)}), bf16[8,32,2048]{2,1,0:T(8,128)(2,1)}, u32[]{:S(2)}, u32[]{:S(2)}) %all-to-all-start.2) | async-done | bytes 1048608 | tf_op jit(solution)/shard_map/all_to_all | solution.py:90
  97.0 4.4 %all-to-all-start.3 = ((bf16[8,32,2048]{2,1,0:T(8,128)(2,1)}), bf16[8,32,2048]{2,1,0:T(8,128)(2,1)}, u32[]{:S(2)}, u32[]{:S(2)}) async-start(bf16[8,32,2048]{2,1,0:T(8,128)(2,1)} %bitcast.76), calls=%async_computation.3 | async-start | bytes 2097152 | tf_op jit(solution)/shard_map/all_to_all | solution.py:107
  101.5 2.8 %broadcast_multiply_fusion = (bf16[256,2048]{1,0:T(8,128)(2,1)}, f32[256,2048]{1,0:T(8,128)S(1)}) fusion(f32[256]{0:T(256)S(1)} %bitcast.85, bf16[256,2048]{1,0:T(8,128)(2,1)} %bitcast.12, s32[256]{0:T(256)S(1)} %bitcast.82), kind=kOutput, calls=%fused_computation.23 | convolution fusion | flops 269549568 | bytes 4196352 | tf_op jit(solution)/shard_map/dot_general | solution.py:27
  104.3 1.8 %fusion.82 = f32[256,384]{0,1:T(8,128)S(1)} fusion(bf16[256,2048]{1,0:T(8,128)(2,1)} %collective-permute-done.2, bf16[192,2048]{1,0:T(8,128)(2,1)S(1)} %copy-done.5, bf16[192,2048]{1,0:T(8,128)(2,1)S(1)} %copy-done.7), kind=kOutput, calls=%fused_computation.116 | convolution fusion | flops 405798912 | bytes 3014656 | tf_op jit(solution)/shard_map/dot_general | solution.py:15
  106.2 1.8 %fusion.83 = f32[256,384]{0,1:T(8,128)S(1)} fusion(bf16[256,2048]{1,0:T(8,128)(2,1)} %collective-permute-done, bf16[192,2048]{1,0:T(8,128)(2,1)S(1)} %copy-done.5, bf16[192,2048]{1,0:T(8,128)(2,1)S(1)} %copy-done.7), kind=kOutput, calls=%fused_computation.117 | convolution fusion | flops 405798912 | bytes 3014656 | tf_op jit(solution)/shard_map/dot_general | solution.py:15
  108.0 0.6 collective-permute-start.4
  108.6 1.7 %multiply_convert_fusion.11 = (bf16[256,192]{0,1:T(8,128)(2,1)S(1)}, bf16[256,192]{0,1:T(8,128)(2,1)S(1)}) fusion(f32[256,384]{0,1:T(8,128)S(1)} %fusion.82, bf16[256,2048]{1,0:T(8,128)(2,1)} %collective-permute-done.3, bf16[1,768,2048]{2,1,0:T(8,128)(2,1)S(1)} %copy-done, s32[]{:T(128)S(6)} %select_n.28), kind=kOutput, calls=%fused_computation.78 | convolution fusion | flops 201965568 | bytes 2424836 | tf_op jit(solution)/shard_map/dot_general | solution.py:15
  110.3 1.8 %multiply_convert_fusion.13 = (bf16[256,192]{0,1:T(8,128)(2,1)S(1)}, bf16[256,192]{0,1:T(8,128)(2,1)S(1)}) fusion(f32[256,384]{0,1:T(8,128)S(1)} %fusion.83, bf16[256,2048]{1,0:T(8,128)(2,1)} %collective-permute-done.1, bf16[1,768,2048]{2,1,0:T(8,128)(2,1)S(1)} %copy-done, s32[]{:T(128)S(6)} %select_n.28), kind=kOutput, calls=%fused_computation.82 | convolution fusion | flops 201965568 | bytes 2424836 | tf_op jit(solution)/shard_map/dot_general | solution.py:15
  112.2 1.8 %fusion.36 = f32[384,2048]{1,0:T(8,128)S(1)} fusion(bf16[256,2048]{1,0:T(8,128)(2,1)} %collective-permute-done, bf16[256,192]{0,1:T(8,128)(2,1)S(1)} %get-tuple-element.41, bf16[256,192]{0,1:T(8,128)(2,1)S(1)} %get-tuple-element.40), kind=kOutput, calls=%fused_computation.57 | convolution fusion | flops 403046400 | bytes 4390912 | tf_op jit(solution)/shard_map/dot_general | solution.py:21
  114.0 0.3 multiply_reduce_fusion
  114.3 0.7 maximum_maximum_fusion
  115.0 1.8 %fusion.40 = f32[384,2048]{1,0:T(8,128)S(1)} fusion(bf16[256,2048]{1,0:T(8,128)(2,1)} %collective-permute-done.2, bf16[256,192]{0,1:T(8,128)(2,1)S(1)} %get-tuple-element.45, bf16[256,192]{0,1:T(8,128)(2,1)S(1)} %get-tuple-element.44), kind=kOutput, calls=%fused_computation.61 | convolution fusion | flops 403046400 | bytes 4390912 | tf_op jit(solution)/shard_map/dot_general | solution.py:21
  116.8 1.6 %convolution_add_fusion.1 = f32[192,2048]{1,0:T(8,128)S(1)} fusion(f32[192,2048]{1,0:T(8,128)S(1)} %copy-done.2, bf16[256,2048]{1,0:T(8,128)(2,1)} %collective-permute-done.1, f32[256,384]{0,1:T(8,128)S(1)} %fusion.83), kind=kOutput, calls=%fused_computation.10 | convolution fusion | flops 202014720 | bytes 4587520 | tf_op jit(solution)/shard_map/dot_general | solution.py:21
  118.4 0.6 fusion.81
  119.1 0.5 multiply_convert_fusion.9
  119.6 0.4 fusion.59
  120.0 2.7 %fusion.13 = bf16[1,192,2048]{2,1,0:T(8,128)(2,1)} fusion(f32[192,2048]{1,0:T(8,128)S(1)} %fusion.59, f32[192,2048]{1,0:T(8,128)S(1)} %convolution_add_fusion.1, bf16[256,2048]{1,0:T(8,128)(2,1)} %collective-permute-done.3, f32[256,384]{0,1:T(8,128)S(1)} %fusion.82), kind=kOutput, calls=%fused_computation.18 | convolution fusion | flops 202801152 | bytes 5373952 | tf_op jit(solution)/shard_map/dot_general | solution.py:21
  122.7 0.6 add_convert_fusion
  123.3 1.2 slice_bitcast_fusion
  124.5 2.1 %all-to-all-done.3 = bf16[8,32,2048]{2,1,0:T(8,128)(2,1)} async-done(((bf16[8,32,2048]{2,1,0:T(8,128)(2,1)}), bf16[8,32,2048]{2,1,0:T(8,128)(2,1)}, u32[]{:S(2)}, u32[]{:S(2)}) %all-to-all-start.3) | async-done | bytes 1048608 | tf_op jit(solution)/shard_map/all_to_all | solution.py:107
  126.6 2.7 %convolution_convert_fusion = bf16[256,2048]{1,0:T(8,128)(2,1)} fusion(bf16[256,2048]{1,0:T(8,128)(2,1)} %bitcast.14, s32[256]{0:T(256)S(1)} %bitcast.83), kind=kOutput, calls=%fused_computation.13 | convolution fusion | flops 269025280 | bytes 2098176 | tf_op jit(solution)/shard_map/dot_general | solution.py:27
  (36 shorter events, 0.2 us)
Async XLA Ops:
  0.6 51.8 %copy-start = (bf16[1,768,2048]{2,1,0:T(8,128)(2,1)S(1)}, bf16[1,768,2048]{2,1,0:T(8,128)(2,1)}, u32[]{:S(2)}) copy-start(bf16[1,768,2048]{2,1,0:T(8,128)(2,1)} %param.12) | copy-start | bytes 9437188
  4.4 33.1 %all-to-all-start = ((bf16[8,32,2048]{2,1,0:T(8,128)(2,1)}), bf16[8,32,2048]{2,1,0:T(8,128)(2,1)}, u32[]{:S(2)}, u32[]{:S(2)}) async-start(bf16[8,32,2048]{2,1,0:T(8,128)(2,1)} %bitcast.75), calls=%async_computation | async-start | bytes 2097152 | tf_op jit(solution)/shard_map/all_to_all | solution.py:56
  37.5 29.9 %all-to-all-start.1 = ((bf16[8,32,2048]{2,1,0:T(8,128)(2,1)}), bf16[8,32,2048]{2,1,0:T(8,128)(2,1)}, u32[]{:S(2)}, u32[]{:S(2)}) async-start(bf16[8,32,2048]{2,1,0:T(8,128)(2,1)} %bitcast.74), calls=%async_computation.1 | async-start | bytes 2097152 | tf_op jit(solution)/shard_map/all_to_all | solution.py:56
  42.0 5.2 %copy-start.8 = (bf16[1,768,2048]{2,1,0:T(8,128)(2,1)S(1)}, bf16[1,768,2048]{2,1,0:T(8,128)(2,1)}, u32[]{:S(2)}) copy-start(bf16[1,768,2048]{2,1,0:T(8,128)(2,1)} %param.11) | copy-start | bytes 9437188
  45.7 58.6 %collective-permute-start.2 = (bf16[256,2048]{1,0:T(8,128)(2,1)}, bf16[256,2048]{1,0:T(8,128)(2,1)}, u32[]{:S(2)}, u32[]{:S(2)}) collective-permute-start(bf16[256,2048]{1,0:T(8,128)(2,1)} %bitcast.5), channel_id=1, source_target_pairs={{0,16},{8,24},{16,0},{24,8},{1,17},{9,25},{17,1},{25,9},{2,18},{10... | collective-permute-start | bytes 3145736 | tf_op jit(solution)/shard_map/ppermute | solution.py:70
  47.2 54.3 %collective-permute-start = (bf16[256,2048]{1,0:T(8,128)(2,1)}, bf16[256,2048]{1,0:T(8,128)(2,1)}, u32[]{:S(2)}, u32[]{:S(2)}) collective-permute-start(bf16[256,2048]{1,0:T(8,128)(2,1)} %bitcast.5), channel_id=1, source_target_pairs={{0,8},{8,0},{16,24},{24,16},{1,9},{9,1},{17,25},{25,17},{2,10},{10... | collective-permute-start | bytes 3145736 | tf_op jit(solution)/shard_map/ppermute | solution.py:70
  51.2 1.2 copy-start.11
  67.3 29.6 %all-to-all-start.2 = ((bf16[8,32,2048]{2,1,0:T(8,128)(2,1)}), bf16[8,32,2048]{2,1,0:T(8,128)(2,1)}, u32[]{:S(2)}, u32[]{:S(2)}) async-start(bf16[8,32,2048]{2,1,0:T(8,128)(2,1)} %bitcast.77), calls=%async_computation.2 | async-start | bytes 2097152 | tf_op jit(solution)/shard_map/all_to_all | solution.py:90
  71.6 3.1 %copy-start.9 = (bf16[1,768,2048]{2,1,0:T(8,128)(2,1)S(1)}, bf16[1,768,2048]{2,1,0:T(8,128)(2,1)}, u32[]{:S(2)}) copy-start(bf16[1,768,2048]{2,1,0:T(8,128)(2,1)} %param.11) | copy-start | bytes 9437188
  71.6 3.6 %copy-start.10 = (bf16[1,768,2048]{2,1,0:T(8,128)(2,1)S(1)}, bf16[1,768,2048]{2,1,0:T(8,128)(2,1)}, u32[]{:S(2)}) copy-start(bf16[1,768,2048]{2,1,0:T(8,128)(2,1)} %param.10) | copy-start | bytes 9437188
  75.2 4.3 %copy-start.4 = (bf16[192,2048]{1,0:T(8,128)(2,1)S(1)}, bf16[192,2048]{1,0:T(8,128)(2,1)}, u32[]{:S(2)}) copy-start(bf16[192,2048]{1,0:T(8,128)(2,1)} %get-tuple-element.48) | copy-start | bytes 2359300
  75.2 4.3 %copy-start.6 = (bf16[192,2048]{1,0:T(8,128)(2,1)S(1)}, bf16[192,2048]{1,0:T(8,128)(2,1)}, u32[]{:S(2)}) copy-start(bf16[192,2048]{1,0:T(8,128)(2,1)} %get-tuple-element.49) | copy-start | bytes 2359300
  78.1 26.2 %collective-permute-start.3 = (bf16[256,2048]{1,0:T(8,128)(2,1)}, bf16[256,2048]{1,0:T(8,128)(2,1)}, u32[]{:S(2)}, u32[]{:S(2)}) collective-permute-start(bf16[256,2048]{1,0:T(8,128)(2,1)} %bitcast.10), channel_id=1, source_target_pairs={{0,16},{8,24},{16,0},{24,8},{1,17},{9,25},{17,1},{25,9},{2,18},{10... | collective-permute-start | bytes 3145736 | tf_op jit(solution)/shard_map/ppermute | solution.py:70
  79.6 21.9 %collective-permute-start.1 = (bf16[256,2048]{1,0:T(8,128)(2,1)}, bf16[256,2048]{1,0:T(8,128)(2,1)}, u32[]{:S(2)}, u32[]{:S(2)}) collective-permute-start(bf16[256,2048]{1,0:T(8,128)(2,1)} %bitcast.10), channel_id=1, source_target_pairs={{0,8},{8,0},{16,24},{24,16},{1,9},{9,1},{17,25},{25,17},{2,10},{10... | collective-permute-start | bytes 3145736 | tf_op jit(solution)/shard_map/ppermute | solution.py:70
  97.0 29.6 %all-to-all-start.3 = ((bf16[8,32,2048]{2,1,0:T(8,128)(2,1)}), bf16[8,32,2048]{2,1,0:T(8,128)(2,1)}, u32[]{:S(2)}, u32[]{:S(2)}) async-start(bf16[8,32,2048]{2,1,0:T(8,128)(2,1)} %bitcast.76), calls=%async_computation.3 | async-start | bytes 2097152 | tf_op jit(solution)/shard_map/all_to_all | solution.py:107
  101.4 2.9 %copy-start.5 = (bf16[192,2048]{1,0:T(8,128)(2,1)S(1)}, bf16[192,2048]{1,0:T(8,128)(2,1)}, u32[]{:S(2)}) copy-start(bf16[192,2048]{1,0:T(8,128)(2,1)} %get-tuple-element.48) | copy-start | bytes 2359300
  101.4 2.8 %copy-start.7 = (bf16[192,2048]{1,0:T(8,128)(2,1)S(1)}, bf16[192,2048]{1,0:T(8,128)(2,1)}, u32[]{:S(2)}) copy-start(bf16[192,2048]{1,0:T(8,128)(2,1)} %get-tuple-element.49) | copy-start | bytes 2359300
  106.1 12.3 %collective-permute-start.5 = (bf16[256,2048]{1,0:T(8,128)(2,1)}, bf16[256,2048]{1,0:T(8,128)(2,1)S(1)}, u32[]{:S(2)}, u32[]{:S(2)}) collective-permute-start(bf16[256,2048]{1,0:T(8,128)(2,1)} %collective-permute-done.2), channel_id=1, source_target_pairs={{0,8},{8,0},{16,24},{24,16},{1,9},{9,1},{17,25},{25,17},{2,10},{10... | collective-permute-start | bytes 3145736 | tf_op jit(solution)/shard_map/ppermute | solution.py:70
  108.0 11.0 %collective-permute-start.4 = (bf16[256,2048]{1,0:T(8,128)(2,1)}, bf16[256,2048]{1,0:T(8,128)(2,1)S(1)}, u32[]{:S(2)}, u32[]{:S(2)}) collective-permute-start(bf16[256,2048]{1,0:T(8,128)(2,1)} %collective-permute-done.3), channel_id=1, source_target_pairs={{0,8},{8,0},{16,24},{24,16},{1,9},{9,1},{17,25},{25,17},{2,10},{10... | collective-permute-start | bytes 3145736 | tf_op jit(solution)/shard_map/ppermute | solution.py:70
  110.3 3.7 %copy-start.3 = (bf16[256,2048]{1,0:T(8,128)(2,1)S(1)}, bf16[256,2048]{1,0:T(8,128)(2,1)}, u32[]{:S(2)}) copy-start(bf16[256,2048]{1,0:T(8,128)(2,1)} %param.13) | copy-start | bytes 3145732
  114.0 2.8 %copy-start.2 = (f32[192,2048]{1,0:T(8,128)S(1)}, f32[192,2048]{1,0:T(8,128)}, u32[]{:S(2)}) copy-start(f32[192,2048]{1,0:T(8,128)} %fusion.58) | copy-start | bytes 4718596
  120.0 2.7 %copy-start.1 = (f32[384,2048]{1,0:T(8,128)S(1)}, f32[384,2048]{1,0:T(8,128)}, u32[]{:S(2)}) copy-start(f32[384,2048]{1,0:T(8,128)} %fusion.32) | copy-start | bytes 9437188
where the time goes:
time: 130 us; the launch traced here: 129 us
  matrix products  49.9 us (38%)
  waiting for transfers between devices  45.1 us (35%)
  starting transfers between devices  23.8 us (18%)
  local copies, waits for them, and re-layouts  7.6 us (6%)
  other arithmetic  1.94 us (1%)
    all_to_all x2, waiting for transfers between devices, exchange(): lax.all_to_all(rows.reshape(experts, per_pair, feature_width), 'ep', spli...  35.4 us
    dot_general x10, matrix products, rows_times(): lax.dot_general(left, right, (((1,), (1,)), ((), ())), preferred_element_...  19 us
    dot_general x7, matrix products, matmul(): return jnp.dot(left, right, preferred_element_type=jnp.float32)  15.8 us
    dot_general x8, matrix products, inner_rows(): lax.dot_general(left, right, (((0,), (0,)), ((), ())), preferred_element_...  15.1 us
    all_to_all x2, starting transfers between devices, exchange(): lax.all_to_all(rows.reshape(experts, per_pair, feature_width), 'ep', spli...  11.5 us
    all_to_all x1, waiting for transfers between devices, body(): lax.all_to_all(expert_out.reshape(experts, per_pair, feature_width), 'ep'...  7.62 us
    all_to_all x1, starting transfers between devices, body(): lax.all_to_all(token_part.reshape(experts, per_pair, feature_width), 'ep'...  4.41 us
    all_to_all x1, starting transfers between devices, body(): lax.all_to_all(expert_out.reshape(experts, per_pair, feature_width), 'ep'...  4.24 us
  transfers between devices with their start and end apart: 10, of which 4 were waited for; matrix products, arithmetic and copies ran while one was open for 40% of the time, Pallas kernels for 0%

commit v1 on v0

--- a/solution.py
+++ b/solution.py
@@ -4,6 +4,22 @@
 from jax.sharding import PartitionSpec as P
 
 STRIPE = 16
+
+
+def exchange_in_pairs(value, axis, split, join):
+    ways, here = (lax.axis_size(axis), lax.axis_index(axis))
+    width = value.shape[split] // ways
+    shape = list(value.shape)
+    shape[split] = width
+    height = shape[join]
+    shape[join] = height * ways
+    full = jnp.zeros(shape, value.dtype)
+    for mask in range(ways):
+        part = lax.dynamic_slice_in_dim(value, (here ^ mask) * width, width, axis=split)
+        if mask:
+            part = lax.ppermute(part, axis, [(d, d ^ mask) for d in range(ways)])
+        full = lax.dynamic_update_slice_in_dim(full, part, (here ^ mask) * height, axis=join)
+    return full
 
 
 def silu_grad(value):
@@ -104,12 +120,8 @@
         token_part, grad_out = lax.optimization_barrier((token_part, grad_in))
         far_grad = to_copy(grad_out, 2)
         near_grad = to_copy(grad_out, 1)
-    part_back = lax.all_to_all(
-        token_part.reshape(experts, per_pair, feature_width),
-        "ep",
-        split_axis=0,
-        concat_axis=0,
-        tiled=True,
+    part_back = exchange_in_pairs(
+        token_part.reshape(experts, per_pair, feature_width), "ep", 0, 0
     ).reshape(total_slots, feature_width)
     if by_pieces:
         returned, near_rows, near_grad = lax.optimization_barrier((returned, near_rows, near_grad))

time: 130 us -> 176 us (1.35)
  waiting for transfers between devices: 45.1 us -> 71.9 us
  starting transfers between devices: 23.8 us -> 33.9 us
  local copies, waits for them, and re-layouts: 7.6 us -> 16.2 us
    ppermute x0 -> x7, waiting for transfers between devices: none -> 36.5 us  [exchange_in_pairs(): part = lax.ppermute(part, axis, [(d, d ^ mask) for d in range(ways)])]
    ppermute x0 -> x7, starting transfers between devices: none -> 14.3 us  [exchange_in_pairs(): part = lax.ppermute(part, axis, [(d, d ^ mask) for d in range(ways)])]
    all_to_all x1, waiting for transfers between devices: 7.62 us -> 0.01 us  [body(): lax.all_to_all(expert_out.reshape(experts, per_pair, feature_width), 'ep'...]
    dynamic_update_slice x0 -> x7, local copies, waits for them, and re-layouts: none -> 4.59 us  [exchange_in_pairs(): lax.dynamic_update_slice_in_dim(full, part, (here ^ mask) * height, axis=...]
    all_to_all x1 -> x0, starting transfers between devices: 4.41 us -> none  [body(): lax.all_to_all(token_part.reshape(experts, per_pair, feature_width), 'ep'...]
    all_to_all x1 -> x0, waiting for transfers between devices: 2.11 us -> none  [body(): lax.all_to_all(token_part.reshape(experts, per_pair, feature_width), 'ep'...]
    dynamic_slice x0 -> x1, local copies, waits for them, and re-layouts: none -> 2.05 us  [exchange_in_pairs(): lax.dynamic_slice_in_dim(value, (here ^ mask) * width, width, axis=split)]
  transfers between devices with their start and end apart: 10 -> 16, of which waited for: 4 -> 8; matrix products, arithmetic and copies ran while one was open for 40% -> 30% of each run, Pallas kernels for 0% -> 0%
where the time goes in v1:
time: 176 us; the launch traced here: 175 us
  waiting for transfers between devices  71.9 us (41%)
  matrix products  49.7 us (28%)
  starting transfers between devices  33.9 us (19%)
  local copies, waits for them, and re-layouts  16.2 us (9%)
  other arithmetic  1.94 us (1%)
    ppermute x7, waiting for transfers between devices, exchange_in_pairs(): part = lax.ppermute(part, axis, [(d, d ^ mask) for d in range(ways)])  36.5 us
    all_to_all x2, waiting for transfers between devices, exchange(): lax.all_to_all(rows.reshape(experts, per_pair, feature_width), 'ep', spli...  35.3 us
    dot_general x10, matrix products, rows_times(): lax.dot_general(left, right, (((1,), (1,)), ((), ())), preferred_element_...  19 us
    dot_general x7, matrix products, matmul(): return jnp.dot(left, right, preferred_element_type=jnp.float32)  15.7 us
    dot_general x8, matrix products, inner_rows(): lax.dot_general(left, right, (((0,), (0,)), ((), ())), preferred_element_...  15 us
    ppermute x7, starting transfers between devices, exchange_in_pairs(): part = lax.ppermute(part, axis, [(d, d ^ mask) for d in range(ways)])  14.3 us
    all_to_all x2, starting transfers between devices, exchange(): lax.all_to_all(rows.reshape(experts, per_pair, feature_width), 'ep', spli...  11.5 us
    dynamic_update_slice x7, local copies, waits for them, and re-layouts, exchange_in_pairs(): lax.dynamic_update_slice_in_dim(full, part, (here ^ mask) * height, axis=...  4.59 us
  transfers between devices with their start and end apart: 16, of which 8 were waited for; matrix products, arithmetic and copies ran while one was open for 30% of the time, Pallas kernels for 0%

profile of v1, /device:TPU:0, one launch (start us, length us, event | category | flops | bytes accessed | tf_op | source)
XLA Modules:
  0.0 174.6 jit_solution(5577957261565460617)
XLA Ops:
  0.6 0.9 slice.45
  1.7 2.6 %convolution_convert_fusion.1 = bf16[256,2048]{1,0:T(8,128)(2,1)} fusion(bf16[256,2048]{1,0:T(8,128)(2,1)} %param.7, s32[256]{0:T(256)S(1)} %compare_select_fusion.1), kind=kOutput, calls=%fused_computation.14 | convolution fusion | flops 269025280 | bytes 2098176 | tf_op jit(solution)/shard_map/dot_general | solution.py:43
  4.4 7.3 %all-to-all-start = ((bf16[8,32,2048]{2,1,0:T(8,128)(2,1)}), bf16[8,32,2048]{2,1,0:T(8,128)(2,1)}, u32[]{:S(2)}, u32[]{:S(2)}) async-start(bf16[8,32,2048]{2,1,0:T(8,128)(2,1)} %bitcast.75), calls=%async_computation | async-start | bytes 2097152 | tf_op jit(solution)/shard_map/all_to_all | solution.py:72
  11.6 0.7 slice.44
  12.4 2.6 %fusion.6 = bf16[256,2048]{1,0:T(8,128)(2,1)} fusion(bf16[256,2048]{1,0:T(8,128)(2,1)} %param.13, f32[256]{0:T(256)S(1)} %select_reduce_fusion, s32[256]{0:T(256)S(1)} %compare_select_fusion.1), kind=kOutput, calls=%fused_computation.11 | convolution fusion | flops 269549568 | bytes 2099200 | tf_op jit(solution)/shard_map/dot_general | solution.py:43
  15.1 22.4 %all-to-all-done = bf16[8,32,2048]{2,1,0:T(8,128)(2,1)} async-done(((bf16[8,32,2048]{2,1,0:T(8,128)(2,1)}), bf16[8,32,2048]{2,1,0:T(8,128)(2,1)}, u32[]{:S(2)}, u32[]{:S(2)}) %all-to-all-start) | async-done | bytes 1048608 | tf_op jit(solution)/shard_map/all_to_all | solution.py:72
  37.5 4.2 %all-to-all-start.1 = ((bf16[8,32,2048]{2,1,0:T(8,128)(2,1)}), bf16[8,32,2048]{2,1,0:T(8,128)(2,1)}, u32[]{:S(2)}, u32[]{:S(2)}) async-start(bf16[8,32,2048]{2,1,0:T(8,128)(2,1)} %bitcast.74), calls=%async_computation.1 | async-start | bytes 2097152 | tf_op jit(solution)/shard_map/all_to_all | solution.py:72
  42.0 0.9 compare_select_fusion
  42.9 2.8 %dynamic-slice_bitcast_fusion = (bf16[192,2048]{1,0:T(8,128)(2,1)}, bf16[192,2048]{1,0:T(8,128)(2,1)}) fusion(bf16[1,768,2048]{2,1,0:T(8,128)(2,1)} %param.11, s32[]{:T(128)S(6)} %select_n.68, bf16[1,768,2048]{2,1,0:T(8,128)(2,1)} %param.10), kind=kLoop, calls=%fused_computation.37 | loop fusion | bytes 3145732 | tf_op jit(solution)/shard_map/dynamic_slice | solution.py:155
  45.7 1.5 collective-permute-start.2
  47.2 4.0 %fusion.1 = f32[256,1536]{1,0:T(8,128)S(1)} fusion(bf16[256,2048]{1,0:T(8,128)(2,1)} %bitcast.5, bf16[768,2048]{1,0:T(8,128)(2,1)S(1)} %bitcast.78, bf16[768,2048]{1,0:T(8,128)(2,1)} %bitcast.80), kind=kOutput, calls=%fused_computation.2 | convolution fusion | flops 1623195648 | bytes 8912896 | tf_op jit(solution)/shard_map/dot_general | solution.py:31
  51.2 1.2 copy-done.11
  52.4 2.0 %fusion.9 = bf16[256,2048]{1,0:T(8,128)(2,1)} fusion(bf16[1,768,2048]{2,1,0:T(8,128)(2,1)S(1)} %copy-done, f32[256,1536]{1,0:T(8,128)S(1)} %fusion.1), kind=kOutput, calls=%fused_computation.16 | convolution fusion | flops 807010304 | bytes 5767168 | tf_op jit(solution)/shard_map/dot_general | solution.py:43
  54.5 12.9 %all-to-all-done.1 = bf16[8,32,2048]{2,1,0:T(8,128)(2,1)} async-done(((bf16[8,32,2048]{2,1,0:T(8,128)(2,1)}), bf16[8,32,2048]{2,1,0:T(8,128)(2,1)}, u32[]{:S(2)}, u32[]{:S(2)}) %all-to-all-start.1) | async-done | bytes 1048608 | tf_op jit(solution)/shard_map/all_to_all | solution.py:72
  67.3 3.0 %multiply_convert_fusion.1 = (bf16[256,768]{1,0:T(8,128)(2,1)S(1)}, bf16[256,768]{1,0:T(8,128)(2,1)S(1)}) fusion(f32[256,1536]{1,0:T(8,128)} %copy-done.11, bf16[256,2048]{1,0:T(8,128)(2,1)} %bitcast.10, bf16[1,768,2048]{2,1,0:T(8,128)(2,1)S(1)} %copy-done), kind=kOutput, calls=%fused_computation.40 | convolution fusion | flops 807862272 | bytes 6553600 | tf_op jit(solution)/shard_map/dot_general | solution.py:31
  71.0 2.8 %fusion.7 = bf16[256,2048]{1,0:T(8,128)(2,1)} fusion(bf16[768,2048]{1,0:T(8,128)(2,1)S(1)} %bitcast.79, bf16[768,2048]{1,0:T(8,128)(2,1)S(1)} %bitcast.81, bf16[256,768]{1,0:T(8,128)(2,1)S(1)} %get-tuple-element.35, bf16[256,768]{1,0:T(8,128)(2,1)S(1)} %get-tuple-element.34), kind=kOutput, calls=%fused_computation.12 | convolution fusion | flops 1625292800 | bytes 8126464 | tf_op jit(solution)/shard_map/dot_general | solution.py:43
  73.7 1.5 collective-permute-start.3
  75.3 4.4 %all-to-all-start.2 = ((bf16[8,32,2048]{2,1,0:T(8,128)(2,1)}), bf16[8,32,2048]{2,1,0:T(8,128)(2,1)}, u32[]{:S(2)}, u32[]{:S(2)}) async-start(bf16[8,32,2048]{2,1,0:T(8,128)(2,1)} %bitcast.76), calls=%async_computation.2 | async-start | bytes 2097152 | tf_op jit(solution)/shard_map/all_to_all | solution.py:106
  79.7 1.2 broadcast_in_dim.46
  80.9 2.0 %constant_dynamic-slice_fusion = (bf16[1,32,2048]{2,1,0:T(8,128)(2,1)S(1)}, bf16[1,32,2048]{2,1,0:T(8,128)(2,1)S(1)}, bf16[1,32,2048]{2,1,0:T(8,128)(2,1)S(1)}, ...) fusion(bf16[8,32,2048]{2,1,0:T(8,128)(2,1)} %bitcast.77, ...), kind=kLoop, calls=%fused_computation.102 | loop fusion | bytes 2097184 | tf_op jit(solution)/shard_map/dynamic_slice | solution.py:18
  82.9 1.7 collective-permute-start.4
  84.6 1.8 %fusion.84 = f32[256,384]{0,1:T(8,128)S(1)} fusion(bf16[256,2048]{1,0:T(8,128)(2,1)} %bitcast.5, bf16[192,2048]{1,0:T(8,128)(2,1)S(1)} %copy-done.4, bf16[192,2048]{1,0:T(8,128)(2,1)S(1)} %copy-done.6), kind=kOutput, calls=%fused_computation.133 | convolution fusion | flops 405798912 | bytes 3014656 | tf_op jit(solution)/shard_map/dot_general | solution.py:31
  86.5 1.7 multiply_convert_fusion.15
  88.2 3.4 %fusion.32 = f32[384,2048]{1,0:T(8,128)} fusion(bf16[256,2048]{1,0:T(8,128)(2,1)} %bitcast.5, bf16[256,192]{0,1:T(8,128)(2,1)S(1)} %get-tuple-element.51, bf16[256,192]{0,1:T(8,128)(2,1)S(1)} %get-tuple-element.50), kind=kOutput, calls=%fused_computation.53 | convolution fusion | flops 403046400 | bytes 4390912 | tf_op jit(solution)/shard_map/dot_general | solution.py:37
  91.6 2.8 %fusion.58 = f32[192,2048]{1,0:T(8,128)} fusion(bf16[256,2048]{1,0:T(8,128)(2,1)} %bitcast.10, f32[256,384]{0,1:T(8,128)S(1)} %fusion.84), kind=kOutput, calls=%fused_computation.94 | convolution fusion | flops 201621504 | bytes 3014656 | tf_op jit(solution)/shard_map/dot_general | solution.py:37
  94.4 1.5 collective-permute-start.5
  96.6 4.9 %collective-permute-done.5 = bf16[1,32,2048]{2,1,0:T(8,128)(2,1)S(1)} collective-permute-done((bf16[1,32,2048]{2,1,0:T(8,128)(2,1)S(1)}, bf16[1,32,2048]{2,1,0:T(8,128)(2,1)S(1)}, u32[]{:S(2)}, u32[]{:S(2)}) %collective-permute-start.5) | collective-permute-done | bytes 131104 | tf_op jit(solution)/shard_map/ppermute | solution.py:20
  101.5 3.0 %collective-permute-start.6 = (bf16[1,32,2048]{2,1,0:T(8,128)(2,1)S(1)}, bf16[1,32,2048]{2,1,0:T(8,128)(2,1)S(1)}, u32[]{:S(2)}, u32[]{:S(2)}) collective-permute-start(bf16[1,32,2048]{2,1,0:T(8,128)(2,1)S(1)} %get-tuple-element.42), channel_id=1, source_target_pairs={{0,3},{1,2},{2,1},{3,0},{4,7},{5,6},{6,5},{7,4},{8,11},{9,10},{10,... | collective-permute-start | bytes 393224 | tf_op jit(solution)/shard_map/ppermute | solution.py:20
  105.1 4.7 %collective-permute-done.6 = bf16[1,32,2048]{2,1,0:T(8,128)(2,1)S(1)} collective-permute-done((bf16[1,32,2048]{2,1,0:T(8,128)(2,1)S(1)}, bf16[1,32,2048]{2,1,0:T(8,128)(2,1)S(1)}, u32[]{:S(2)}, u32[]{:S(2)}) %collective-permute-start.6) | collective-permute-done | bytes 131104 | tf_op jit(solution)/shard_map/ppermute | solution.py:20
  109.9 6.3 %collective-permute-start.7 = (bf16[1,32,2048]{2,1,0:T(8,128)(2,1)S(1)}, bf16[1,32,2048]{2,1,0:T(8,128)(2,1)S(1)}, u32[]{:S(2)}, u32[]{:S(2)}) collective-permute-start(bf16[1,32,2048]{2,1,0:T(8,128)(2,1)S(1)} %get-tuple-element.41), channel_id=1, source_target_pairs={{0,4},{1,5},{2,6},{3,7},{4,0},{5,1},{6,2},{7,3},{8,12},{9,13},{10,... | collective-permute-start | bytes 393224 | tf_op jit(solution)/shard_map/ppermute | solution.py:20
  116.8 5.5 %collective-permute-done.7 = bf16[1,32,2048]{2,1,0:T(8,128)(2,1)S(1)} collective-permute-done((bf16[1,32,2048]{2,1,0:T(8,128)(2,1)S(1)}, bf16[1,32,2048]{2,1,0:T(8,128)(2,1)S(1)}, u32[]{:S(2)}, u32[]{:S(2)}) %collective-permute-start.7) | collective-permute-done | bytes 131104 | tf_op jit(solution)/shard_map/ppermute | solution.py:20
  123.2 9.9 %collective-permute-done.8 = bf16[1,32,2048]{2,1,0:T(8,128)(2,1)S(1)} collective-permute-done((bf16[1,32,2048]{2,1,0:T(8,128)(2,1)S(1)}, bf16[1,32,2048]{2,1,0:T(8,128)(2,1)S(1)}, u32[]{:S(2)}, u32[]{:S(2)}) %collective-permute-start.8) | collective-permute-done | bytes 131104 | tf_op jit(solution)/shard_map/ppermute | solution.py:20
  134.2 5.7 %collective-permute-done.9 = bf16[1,32,2048]{2,1,0:T(8,128)(2,1)S(1)} collective-permute-done((bf16[1,32,2048]{2,1,0:T(8,128)(2,1)S(1)}, bf16[1,32,2048]{2,1,0:T(8,128)(2,1)S(1)}, u32[]{:S(2)}, u32[]{:S(2)}) %collective-permute-start.9) | collective-permute-done | bytes 131104 | tf_op jit(solution)/shard_map/ppermute | solution.py:20
  139.9 1.1 collective-permute-start.10
  141.7 5.9 %collective-permute-done.10 = bf16[1,32,2048]{2,1,0:T(8,128)(2,1)S(1)} collective-permute-done((bf16[1,32,2048]{2,1,0:T(8,128)(2,1)S(1)}, bf16[1,32,2048]{2,1,0:T(8,128)(2,1)S(1)}, u32[]{:S(2)}, u32[]{:S(2)}) %collective-permute-start.10) | collective-permute-done | bytes 131104 | tf_op jit(solution)/shard_map/ppermute | solution.py:20
  148.2 2.8 %broadcast_multiply_fusion = (bf16[256,2048]{1,0:T(8,128)(2,1)}, f32[256,2048]{1,0:T(8,128)S(1)}) fusion(f32[256]{0:T(256)S(1)} %bitcast.85, bf16[256,2048]{1,0:T(8,128)(2,1)} %bitcast.12, s32[256]{0:T(256)S(1)} %bitcast.82), kind=kOutput, calls=%fused_computation.23 | convolution fusion | flops 269549568 | bytes 4196352 | tf_op jit(solution)/shard_map/dot_general | solution.py:43
  151.1 1.8 %fusion.82 = f32[256,384]{0,1:T(8,128)S(1)} fusion(bf16[256,2048]{1,0:T(8,128)(2,1)} %collective-permute-done.2, bf16[192,2048]{1,0:T(8,128)(2,1)S(1)} %copy-done.5, bf16[192,2048]{1,0:T(8,128)(2,1)S(1)} %copy-done.7), kind=kOutput, calls=%fused_computation.131 | convolution fusion | flops 405798912 | bytes 3014656 | tf_op jit(solution)/shard_map/dot_general | solution.py:31
  153.0 1.8 %fusion.83 = f32[256,384]{0,1:T(8,128)S(1)} fusion(bf16[256,2048]{1,0:T(8,128)(2,1)} %collective-permute-done, bf16[192,2048]{1,0:T(8,128)(2,1)S(1)} %copy-done.5, bf16[192,2048]{1,0:T(8,128)(2,1)S(1)} %copy-done.7), kind=kOutput, calls=%fused_computation.132 | convolution fusion | flops 405798912 | bytes 3014656 | tf_op jit(solution)/shard_map/dot_general | solution.py:31
  155.4 1.7 multiply_convert_fusion.11
  157.1 1.8 %multiply_convert_fusion.13 = (bf16[256,192]{0,1:T(8,128)(2,1)S(1)}, bf16[256,192]{0,1:T(8,128)(2,1)S(1)}) fusion(f32[256,384]{0,1:T(8,128)S(1)} %fusion.83, bf16[256,2048]{1,0:T(8,128)(2,1)} %collective-permute-done.1, bf16[1,768,2048]{2,1,0:T(8,128)(2,1)S(1)} %copy-done, s32[]{:T(128)S(6)} %select_n.68), kind=kOutput, calls=%fused_computation.82 | convolution fusion | flops 201965568 | bytes 2424836 | tf_op jit(solution)/shard_map/dot_general | solution.py:31
  158.9 1.8 %fusion.36 = f32[384,2048]{1,0:T(8,128)S(1)} fusion(bf16[256,2048]{1,0:T(8,128)(2,1)} %collective-permute-done, bf16[256,192]{0,1:T(8,128)(2,1)S(1)} %get-tuple-element.49, bf16[256,192]{0,1:T(8,128)(2,1)S(1)} %get-tuple-element.48), kind=kOutput, calls=%fused_computation.57 | convolution fusion | flops 403046400 | bytes 4390912 | tf_op jit(solution)/shard_map/dot_general | solution.py:37
  161.1 0.7 maximum_maximum_fusion
  161.7 1.8 %fusion.40 = f32[384,2048]{1,0:T(8,128)S(1)} fusion(bf16[256,2048]{1,0:T(8,128)(2,1)} %collective-permute-done.2, bf16[256,192]{0,1:T(8,128)(2,1)S(1)} %get-tuple-element.53, bf16[256,192]{0,1:T(8,128)(2,1)S(1)} %get-tuple-element.52), kind=kOutput, calls=%fused_computation.61 | convolution fusion | flops 403046400 | bytes 4390912 | tf_op jit(solution)/shard_map/dot_general | solution.py:37
  163.6 1.6 convolution_add_fusion.1
  166.3 0.7 copy-done.1
  167.7 1.2 slice_bitcast_fusion
  169.3 2.6 %fusion.13 = bf16[1,192,2048]{2,1,0:T(8,128)(2,1)} fusion(f32[192,2048]{1,0:T(8,128)S(1)} %fusion.59, f32[192,2048]{1,0:T(8,128)S(1)} %convolution_add_fusion.1, bf16[256,2048]{1,0:T(8,128)(2,1)} %collective-permute-done.3, f32[256,384]{0,1:T(8,128)S(1)} %fusion.82), kind=kOutput, calls=%fused_computation.18 | convolution fusion | flops 202801152 | bytes 5373952 | tf_op jit(solution)/shard_map/dot_general | solution.py:37
  171.9 2.7 %convolution_convert_fusion = bf16[256,2048]{1,0:T(8,128)(2,1)} fusion(bf16[256,2048]{1,0:T(8,128)(2,1)} %bitcast.14, s32[256]{0:T(256)S(1)} %bitcast.83), kind=kOutput, calls=%fused_computation.13 | convolution fusion | flops 269025280 | bytes 2098176 | tf_op jit(solution)/shard_map/dot_general | solution.py:43
  (57 shorter events, 9.6 us)
Async XLA Ops:
  0.6 51.8 %copy-start = (bf16[1,768,2048]{2,1,0:T(8,128)(2,1)S(1)}, bf16[1,768,2048]{2,1,0:T(8,128)(2,1)}, u32[]{:S(2)}) copy-start(bf16[1,768,2048]{2,1,0:T(8,128)(2,1)} %param.12) | copy-start | bytes 9437188
  4.4 33.1 %all-to-all-start = ((bf16[8,32,2048]{2,1,0:T(8,128)(2,1)}), bf16[8,32,2048]{2,1,0:T(8,128)(2,1)}, u32[]{:S(2)}, u32[]{:S(2)}) async-start(bf16[8,32,2048]{2,1,0:T(8,128)(2,1)} %bitcast.75), calls=%async_computation | async-start | bytes 2097152 | tf_op jit(solution)/shard_map/all_to_all | solution.py:72
  37.5 29.9 %all-to-all-start.1 = ((bf16[8,32,2048]{2,1,0:T(8,128)(2,1)}), bf16[8,32,2048]{2,1,0:T(8,128)(2,1)}, u32[]{:S(2)}, u32[]{:S(2)}) async-start(bf16[8,32,2048]{2,1,0:T(8,128)(2,1)} %bitcast.74), calls=%async_computation.1 | async-start | bytes 2097152 | tf_op jit(solution)/shard_map/all_to_all | solution.py:72
  42.0 5.2 %copy-start.8 = (bf16[1,768,2048]{2,1,0:T(8,128)(2,1)S(1)}, bf16[1,768,2048]{2,1,0:T(8,128)(2,1)}, u32[]{:S(2)}) copy-start(bf16[1,768,2048]{2,1,0:T(8,128)(2,1)} %param.11) | copy-start | bytes 9437188
  45.7 105.4 %collective-permute-start.2 = (bf16[256,2048]{1,0:T(8,128)(2,1)}, bf16[256,2048]{1,0:T(8,128)(2,1)}, u32[]{:S(2)}, u32[]{:S(2)}) collective-permute-start(bf16[256,2048]{1,0:T(8,128)(2,1)} %bitcast.5), channel_id=1, source_target_pairs={{0,16},{8,24},{16,0},{24,8},{1,17},{9,25},{17,1},{25,9},{2,18},{10... | collective-permute-start | bytes 3145736 | tf_op jit(solution)/shard_map/ppermute | solution.py:86
  47.2 101.0 %collective-permute-start = (bf16[256,2048]{1,0:T(8,128)(2,1)}, bf16[256,2048]{1,0:T(8,128)(2,1)}, u32[]{:S(2)}, u32[]{:S(2)}) collective-permute-start(bf16[256,2048]{1,0:T(8,128)(2,1)} %bitcast.5), channel_id=1, source_target_pairs={{0,8},{8,0},{16,24},{24,16},{1,9},{9,1},{17,25},{25,17},{2,10},{10... | collective-permute-start | bytes 3145736 | tf_op jit(solution)/shard_map/ppermute | solution.py:86
  51.2 1.2 copy-start.11
  67.3 3.0 %copy-start.9 = (bf16[1,768,2048]{2,1,0:T(8,128)(2,1)S(1)}, bf16[1,768,2048]{2,1,0:T(8,128)(2,1)}, u32[]{:S(2)}) copy-start(bf16[1,768,2048]{2,1,0:T(8,128)(2,1)} %param.11) | copy-start | bytes 9437188
  67.3 3.6 %copy-start.10 = (bf16[1,768,2048]{2,1,0:T(8,128)(2,1)S(1)}, bf16[1,768,2048]{2,1,0:T(8,128)(2,1)}, u32[]{:S(2)}) copy-start(bf16[1,768,2048]{2,1,0:T(8,128)(2,1)} %param.10) | copy-start | bytes 9437188
  73.7 77.3 %collective-permute-start.3 = (bf16[256,2048]{1,0:T(8,128)(2,1)}, bf16[256,2048]{1,0:T(8,128)(2,1)}, u32[]{:S(2)}, u32[]{:S(2)}) collective-permute-start(bf16[256,2048]{1,0:T(8,128)(2,1)} %bitcast.10), channel_id=1, source_target_pairs={{0,16},{8,24},{16,0},{24,8},{1,17},{9,25},{17,1},{25,9},{2,18},{10... | collective-permute-start | bytes 3145736 | tf_op jit(solution)/shard_map/ppermute | solution.py:86
  75.3 72.9 %collective-permute-start.1 = (bf16[256,2048]{1,0:T(8,128)(2,1)}, bf16[256,2048]{1,0:T(8,128)(2,1)}, u32[]{:S(2)}, u32[]{:S(2)}) collective-permute-start(bf16[256,2048]{1,0:T(8,128)(2,1)} %bitcast.10), channel_id=1, source_target_pairs={{0,8},{8,0},{16,24},{24,16},{1,9},{9,1},{17,25},{25,17},{2,10},{10... | collective-permute-start | bytes 3145736 | tf_op jit(solution)/shard_map/ppermute | solution.py:86
  75.3 72.9 %all-to-all-start.2 = ((bf16[8,32,2048]{2,1,0:T(8,128)(2,1)}), bf16[8,32,2048]{2,1,0:T(8,128)(2,1)}, u32[]{:S(2)}, u32[]{:S(2)}) async-start(bf16[8,32,2048]{2,1,0:T(8,128)(2,1)} %bitcast.76), calls=%async_computation.2 | async-start | bytes 2097152 | tf_op jit(solution)/shard_map/all_to_all | solution.py:106
  79.7 4.9 %copy-start.4 = (bf16[192,2048]{1,0:T(8,128)(2,1)S(1)}, bf16[192,2048]{1,0:T(8,128)(2,1)}, u32[]{:S(2)}) copy-start(bf16[192,2048]{1,0:T(8,128)(2,1)} %get-tuple-element.56) | copy-start | bytes 2359300
  79.7 4.9 %copy-start.6 = (bf16[192,2048]{1,0:T(8,128)(2,1)S(1)}, bf16[192,2048]{1,0:T(8,128)(2,1)}, u32[]{:S(2)}) copy-start(bf16[192,2048]{1,0:T(8,128)(2,1)} %get-tuple-element.57) | copy-start | bytes 2359300
  82.9 11.5 %collective-permute-start.4 = (bf16[1,32,2048]{2,1,0:T(8,128)(2,1)S(1)}, bf16[1,32,2048]{2,1,0:T(8,128)(2,1)S(1)}, u32[]{:S(2)}, u32[]{:S(2)}) collective-permute-start(bf16[1,32,2048]{2,1,0:T(8,128)(2,1)S(1)} %get-tuple-element.44), channel_id=1, source_target_pairs={{0,1},{1,0},{2,3},{3,2},{4,5},{5,4},{6,7},{7,6},{8,9},{9,8},{10,11... | collective-permute-start | bytes 393224 | tf_op jit(solution)/shard_map/ppermute | solution.py:20
  94.4 7.0 %collective-permute-start.5 = (bf16[1,32,2048]{2,1,0:T(8,128)(2,1)S(1)}, bf16[1,32,2048]{2,1,0:T(8,128)(2,1)S(1)}, u32[]{:S(2)}, u32[]{:S(2)}) collective-permute-start(bf16[1,32,2048]{2,1,0:T(8,128)(2,1)S(1)} %get-tuple-element.43), channel_id=1, source_target_pairs={{0,2},{1,3},{2,0},{3,1},{4,6},{5,7},{6,4},{7,5},{8,10},{9,11},{10,... | collective-permute-start | bytes 393224 | tf_op jit(solution)/shard_map/ppermute | solution.py:20
  101.5 8.4 %collective-permute-start.6 = (bf16[1,32,2048]{2,1,0:T(8,128)(2,1)S(1)}, bf16[1,32,2048]{2,1,0:T(8,128)(2,1)S(1)}, u32[]{:S(2)}, u32[]{:S(2)}) collective-permute-start(bf16[1,32,2048]{2,1,0:T(8,128)(2,1)S(1)} %get-tuple-element.42), channel_id=1, source_target_pairs={{0,3},{1,2},{2,1},{3,0},{4,7},{5,6},{6,5},{7,4},{8,11},{9,10},{10,... | collective-permute-start | bytes 393224 | tf_op jit(solution)/shard_map/ppermute | solution.py:20
  109.9 12.4 %collective-permute-start.7 = (bf16[1,32,2048]{2,1,0:T(8,128)(2,1)S(1)}, bf16[1,32,2048]{2,1,0:T(8,128)(2,1)S(1)}, u32[]{:S(2)}, u32[]{:S(2)}) collective-permute-start(bf16[1,32,2048]{2,1,0:T(8,128)(2,1)S(1)} %get-tuple-element.41), channel_id=1, source_target_pairs={{0,4},{1,5},{2,6},{3,7},{4,0},{5,1},{6,2},{7,3},{8,12},{9,13},{10,... | collective-permute-start | bytes 393224 | tf_op jit(solution)/shard_map/ppermute | solution.py:20
  122.3 10.8 %collective-permute-start.8 = (bf16[1,32,2048]{2,1,0:T(8,128)(2,1)S(1)}, bf16[1,32,2048]{2,1,0:T(8,128)(2,1)S(1)}, u32[]{:S(2)}, u32[]{:S(2)}) collective-permute-start(bf16[1,32,2048]{2,1,0:T(8,128)(2,1)S(1)} %get-tuple-element.40), channel_id=1, source_target_pairs={{0,5},{1,4},{2,7},{3,6},{4,1},{5,0},{6,3},{7,2},{8,13},{9,12},{10,... | collective-permute-start | bytes 393224 | tf_op jit(solution)/shard_map/ppermute | solution.py:20
  133.1 6.8 %collective-permute-start.9 = (bf16[1,32,2048]{2,1,0:T(8,128)(2,1)S(1)}, bf16[1,32,2048]{2,1,0:T(8,128)(2,1)S(1)}, u32[]{:S(2)}, u32[]{:S(2)}) collective-permute-start(bf16[1,32,2048]{2,1,0:T(8,128)(2,1)S(1)} %get-tuple-element.39), channel_id=1, source_target_pairs={{0,6},{1,7},{2,4},{3,5},{4,2},{5,3},{6,0},{7,1},{8,14},{9,15},{10,... | collective-permute-start | bytes 393224 | tf_op jit(solution)/shard_map/ppermute | solution.py:20
  139.9 7.7 %collective-permute-start.10 = (bf16[1,32,2048]{2,1,0:T(8,128)(2,1)S(1)}, bf16[1,32,2048]{2,1,0:T(8,128)(2,1)S(1)}, u32[]{:S(2)}, u32[]{:S(2)}) collective-permute-start(bf16[1,32,2048]{2,1,0:T(8,128)(2,1)S(1)} %get-tuple-element.38), channel_id=1, source_target_pairs={{0,7},{1,6},{2,5},{3,4},{4,3},{5,2},{6,1},{7,0},{8,15},{9,14},{10,... | collective-permute-start | bytes 393224 | tf_op jit(solution)/shard_map/ppermute | solution.py:20
  148.2 2.8 %copy-start.5 = (bf16[192,2048]{1,0:T(8,128)(2,1)S(1)}, bf16[192,2048]{1,0:T(8,128)(2,1)}, u32[]{:S(2)}) copy-start(bf16[192,2048]{1,0:T(8,128)(2,1)} %get-tuple-element.56) | copy-start | bytes 2359300
  148.2 2.8 %copy-start.7 = (bf16[192,2048]{1,0:T(8,128)(2,1)S(1)}, bf16[192,2048]{1,0:T(8,128)(2,1)}, u32[]{:S(2)}) copy-start(bf16[192,2048]{1,0:T(8,128)(2,1)} %get-tuple-element.57) | copy-start | bytes 2359300
  152.9 12.3 %collective-permute-start.12 = (bf16[256,2048]{1,0:T(8,128)(2,1)}, bf16[256,2048]{1,0:T(8,128)(2,1)S(1)}, u32[]{:S(2)}, u32[]{:S(2)}) collective-permute-start(bf16[256,2048]{1,0:T(8,128)(2,1)} %collective-permute-done.2), channel_id=1, source_target_pairs={{0,8},{8,0},{16,24},{24,16},{1,9},{9,1},{17,25},{25,17},{2,10},{10... | collective-permute-start | bytes 3145736 | tf_op jit(solution)/shard_map/ppermute | solution.py:86
  154.8 11.0 %collective-permute-start.11 = (bf16[256,2048]{1,0:T(8,128)(2,1)}, bf16[256,2048]{1,0:T(8,128)(2,1)S(1)}, u32[]{:S(2)}, u32[]{:S(2)}) collective-permute-start(bf16[256,2048]{1,0:T(8,128)(2,1)} %collective-permute-done.3), channel_id=1, source_target_pairs={{0,8},{8,0},{16,24},{24,16},{1,9},{9,1},{17,25},{25,17},{2,10},{10... | collective-permute-start | bytes 3145736 | tf_op jit(solution)/shard_map/ppermute | solution.py:86
  157.1 3.7 %copy-start.3 = (bf16[256,2048]{1,0:T(8,128)(2,1)S(1)}, bf16[256,2048]{1,0:T(8,128)(2,1)}, u32[]{:S(2)}) copy-start(bf16[256,2048]{1,0:T(8,128)(2,1)} %param.13) | copy-start | bytes 3145732
  160.8 2.8 %copy-start.2 = (f32[192,2048]{1,0:T(8,128)S(1)}, f32[192,2048]{1,0:T(8,128)}, u32[]{:S(2)}) copy-start(f32[192,2048]{1,0:T(8,128)} %fusion.58) | copy-start | bytes 4718596
  165.2 1.9 %copy-start.1 = (f32[384,2048]{1,0:T(8,128)S(1)}, f32[384,2048]{1,0:T(8,128)}, u32[]{:S(2)}) copy-start(f32[384,2048]{1,0:T(8,128)} %fusion.32) | copy-start | bytes 9437188
